TPU v7x, 32 devices: a whole 2x2x4 slice. The times are simulated.
32 devices in a mesh: seq: 4 (over y, x), tp: 8 (over z, core).
Axes of the slice: x: 2, y: 2, z: 4, core: 2. Of those that a mesh axis runs over, the one named last changes fastest.
Arguments:
- streams: bfloat16 [3, 4096, 1024], P(None, 'tp', 'seq'), may hold values from -6 to 6
- feat_weight: float32 [3, 4096, 7], P(None, 'tp'), may hold values from -2 to 2
- long_filter: float32 [4096, 128], P('tp'), may hold values from -0.5 to 0.5
- skip_gain: float32 [4096], P('tp'), may hold values from -1 to 1
- out_weight: bfloat16 [4096, 4096], P('tp', 'seq'), may hold values from -0.125 to 0.125
- out_grad: bfloat16 [4096, 1024], P('tp', 'seq'), may hold values from -6 to 6
Outputs:
- mixed: bfloat16 [4096, 1024], P('tp', 'seq')
- stream_grad: bfloat16 [3, 4096, 1024], P(None, 'tp', 'seq')
- weight_grad: bfloat16 [4096, 4096], P('tp', 'seq')
All inputs are finite; a program needn't handle non-finite values.
Results may differ from a plain program's by a relative error of at most 0.009.
Values may be sent and summed in bfloat16 or wider, within the bound.
No kernel may reach another device: no remote copies, remote signals or barrier semaphores. Data moves between devices by JAX's collectives and lax.ppermute only.
A program may use at most 64 MiB of HBM per device.

v0:
```python
import math
import jax
import jax.numpy as jnp
from jax import lax
from jax.sharding import PartitionSpec as P


def extended(block, sides, width):
    for axis, dim in sides:
        count = lax.axis_size(axis)
        forward = [(i, i + 1) for i in range(count - 1)]
        backward = [(target, source) for source, target in forward]
        low = lax.ppermute(
            lax.slice_in_dim(block, block.shape[dim] - width, None, axis=dim), axis, forward
        )
        high = lax.ppermute(lax.slice_in_dim(block, 0, width, axis=dim), axis, backward)
        block = jnp.concatenate([low, block, high], axis=dim)
    return block


def from_behind(block, axis, distance):
    devices = range(lax.axis_size(axis))
    route = [(i - distance, i) for i in devices if i - distance in devices]
    return lax.ppermute(block, axis, route)


def correlate(signal, taps):
    return lax.conv_general_dilated(
        signal[None],
        taps[:, None, :],
        (1,),
        "VALID",
        dimension_numbers=("NCH", "OIH", "NCH"),
        feature_group_count=signal.shape[0],
        precision=lax.Precision.HIGHEST,
    )[0]


def rows_of_slab(out_grad, n_seq, n_tp):
    rows, length = out_grad.shape
    piece = rows // n_seq
    split = out_grad.reshape(n_seq, piece, length)
    mine = lax.all_to_all(split, "seq", 0, 0)
    mine = jnp.transpose(mine, (1, 0, 2)).reshape(piece, n_seq * length)
    route = []
    for a in range(n_seq):
        for b in range(n_tp):
            flat = n_seq * b + a
            route.append((a * n_tp + b, flat // n_tp * n_tp + flat % n_tp))
    moved = lax.ppermute(mine, ("seq", "tp"), route)
    return lax.all_gather(moved, "tp", axis=0, tiled=True)


def shards(streams, feat_weight, long_filter, skip_gain, out_weight, out_grad):
    channels = streams.shape[1]
    length = streams.shape[2]
    taps_long = long_filter.shape[1]
    taps_short = feat_weight.shape[2]
    n_seq = lax.axis_size("seq")
    n_tp = lax.axis_size("tp")
    reach = taps_long + taps_short - 2
    slab_grad = rows_of_slab(out_grad, n_seq, n_tp)
    slab_width = slab_grad.shape[0]
    partial_grad = jnp.dot(out_weight, slab_grad, preferred_element_type=jnp.float32)
    gated_grad = lax.psum_scatter(partial_grad, "seq", scatter_dimension=1, tiled=True)
    widened = extended(streams, (("seq", 2),), reach).astype(jnp.float32)
    short_taps = feat_weight.reshape(3 * channels, taps_short)
    feats = correlate(
        widened.reshape(3 * channels, length + 2 * reach), short_taps[:, ::-1]
    ).reshape(3, channels, -1)
    query_feat, key_feat, value_feat = (feats[0], feats[1], feats[2])
    product = key_feat * value_feat
    convolved = correlate(product, long_filter[:, ::-1])
    summed = convolved + skip_gain[:, None] * product[:, taps_long - 1 :]
    query_tail = query_feat[:, taps_long - 1 :]
    gated = (query_tail[:, :length] * summed[:, :length]).astype(jnp.bfloat16)
    gated_all = lax.all_gather(gated, "seq", axis=1, tiled=True)
    partial_out = lax.dot_general(
        out_weight, gated_all, (((0,), (0,)), ((), ())), preferred_element_type=jnp.float32
    )
    group = n_tp // n_seq
    out_rows = slab_width // group
    partial_out = (
        partial_out.reshape(group, out_rows, n_seq, length)
        .transpose(0, 2, 1, 3)
        .reshape(n_tp * out_rows, length)
    )
    output_sum = lax.psum_scatter(partial_out, "tp", scatter_dimension=0, tiled=True)
    route = []
    for s in range(n_seq):
        for p in range(n_tp):
            route.append((s * n_tp + p, p % n_seq * n_tp + group * s + p // n_seq))
    mixed = lax.ppermute(output_sum.astype(jnp.bfloat16), ("seq", "tp"), route)
    scale = 1.0 / math.sqrt(length * n_seq)
    terms = lax.dot_general(
        gated_all.reshape(channels, n_seq, length),
        slab_grad.reshape(slab_width, n_seq, length),
        (((2,), (2,)), ((1,), (1,))),
        preferred_element_type=jnp.float32,
    )
    terms = lax.reduce_precision(terms * scale, exponent_bits=8, mantissa_bits=7)
    weight_grad = jnp.sum(terms, axis=0).astype(jnp.bfloat16)
    next_grad = from_behind(gated_grad[:, :reach].astype(jnp.bfloat16), "seq", -1).astype(
        jnp.float32
    )
    grad_ext = jnp.concatenate([gated_grad, next_grad], axis=1)
    conv_grad = grad_ext * query_tail
    keep = length + taps_short - 1
    prod_grad = correlate(conv_grad, long_filter) + skip_gain[:, None] * conv_grad[:, :keep]
    query_grad = grad_ext[:, :keep] * summed[:, :keep]
    key_grad = prod_grad * value_feat[:, taps_long - 1 : taps_long - 1 + keep]
    value_grad = prod_grad * key_feat[:, taps_long - 1 : taps_long - 1 + keep]
    feat_grad = jnp.stack([query_grad, key_grad, value_grad]).reshape(3 * channels, keep)
    stream_grad = correlate(feat_grad, short_taps).reshape(3, channels, length).astype(jnp.bfloat16)
    return (mixed, stream_grad, weight_grad)


def solution(mesh):
    return jax.shard_map(
        shards,
        mesh=mesh,
        in_specs=(
            P(None, "tp", "seq"),
            P(None, "tp", None),
            P("tp", None),
            P("tp"),
            P("tp", "seq"),
            P("tp", "seq"),
        ),
        out_specs=(P("tp", "seq"), P(None, "tp", "seq"), P("tp", "seq")),
        check_vma=False,
    )
```

profile of v0, /device:TPU:4, one launch (start us, length us, event | category | flops | bytes accessed | tf_op | source)
XLA Modules:
  0.0 241.9 jit_solution(13884115816914673931)
XLA Ops:
  7.2 4.4 %all-to-all-start = ((bf16[4,128,256]{2,1,0:T(8,128)(2,1)}), bf16[4,128,256]{2,1,0:T(8,128)(2,1)S(1)}, u32[]{:S(2)}, u32[]{:S(2)}) async-start(bf16[4,128,256]{2,1,0:T(8,128)(2,1)} %bitcast.78), calls=%async_computation.1 | async-start | bytes 524288 | tf_op jit(solution)/shard_map/all_to_all | solution.py:43
  14.4 3.4 %collective-permute-start = (bf16[3,512,133]{1,2,0:T(8,128)(2,1)}, bf16[3,512,133]{1,2,0:T(8,128)(2,1)S(1)}, u32[]{:S(2)}, u32[]{:S(2)}) collective-permute-start(bf16[3,512,133]{1,2,0:T(8,128)(2,1)} %copy.89), channel_id=1, source_target_pairs={{0,8},{8,16},{16,24},{1,9},{9,17},{17,25},{2,10},{10,18},{18,26},{... | collective-permute-start | bytes 1225736 | tf_op jit(solution)/shard_map/ppermute | solution.py:13
  18.8 3.4 %collective-permute-start.1 = (bf16[3,512,133]{1,2,0:T(8,128)(2,1)}, bf16[3,512,133]{1,2,0:T(8,128)(2,1)S(1)}, u32[]{:S(2)}, u32[]{:S(2)}) collective-permute-start(bf16[3,512,133]{1,2,0:T(8,128)(2,1)} %copy.90), channel_id=1, source_target_pairs={{8,0},{16,8},{24,16},{9,1},{17,9},{25,17},{10,2},{18,10},{26,18},{... | collective-permute-start | bytes 1225736 | tf_op jit(solution)/shard_map/ppermute | solution.py:16
  22.3 1.9 collective-permute-start.3
  25.8 7.5 %collective-permute-done = bf16[3,512,133]{1,2,0:T(8,128)(2,1)S(1)} collective-permute-done((bf16[3,512,133]{1,2,0:T(8,128)(2,1)}, bf16[3,512,133]{1,2,0:T(8,128)(2,1)S(1)}, u32[]{:S(2)}, u32[]{:S(2)}) %collective-permute-start) | collective-permute-done | bytes 408608 | tf_op jit(solution)/shard_map/ppermute | solution.py:13
  37.5 2.6 %pad_maximum_fusion = bf16[3,512,522]{2,1,0:T(8,128)(2,1)S(1)} fusion(bf16[3,512,133]{2,1,0:T(8,128)(2,1)} %copy.61, bf16[3,512,256]{2,1,0:T(8,128)(2,1)} %param.6, bf16[3,512,133]{2,1,0:T(8,128)(2,1)} %copy.60), kind=kLoop, calls=%fused_computation.7 | loop fusion | flops 4810752 | bytes 3207168 | tf_op jit(solution)/shard_map/concatenate | solution.py:17
  40.0 2.2 copy.62
  42.3 2.7 %pad = bf16[1536,1,528]{0,2,1:T(8,128)(2,1)} pad(bf16[1536,1,522]{0,2,1:T(8,128)(2,1)} %copy.62, bf16[]{:T(256)} %constant.12), padding=0_0x0_0x0_6 | pad | bytes 3225602 | tf_op jit(solution)/shard_map/broadcast_in_dim;reshape | solution.py:29
  59.2 2.3 reshape.75
  64.7 21.2 %fusion.36 = f32[1,512,389]{1,0,2:T(1,128)S(1)} fusion(f32[1,528,512]{2,0,1:T(1,128)S(1)} %copy-done.9, f32[512,1,128]{0,1,2:T(1,128)S(1)} %copy-done.13), kind=kOutput, calls=%fused_computation.57 | convolution fusion | flops 305922048 | bytes 2140160 | tf_op jit(solution)/shard_map/conv_general_dilated | solution.py:28
  88.0 4.2 %fusion.37 = f32[512,1024]{0,1:T(8,128)} fusion(bf16[512,1024]{1,0:T(8,128)(2,1)S(1)} %copy-done, bf16[1024,1024]{0,1:T(8,128)(2,1)} %all-gather.5.cloned.1.call-done), kind=kOutput, calls=%fused_computation.58 | convolution fusion | flops 1073741824 | bytes 5242880 | tf_op jit(solution)/shard_map/dot_general | solution.py:64
  92.6 29.9 %all-gather.3.cloned.1.call-done = bf16[512,1024]{0,1:T(8,128)(2,1)} async-done(((bf16[512,256]{0,1:T(8,128)(2,1)}), bf16[512,1024]{0,1:T(8,128)(2,1)}) %all-gather.3.cloned.1.call-update) | async-done | bytes 1048592 | tf_op jit(solution)/shard_map/all_gather | solution.py:77
  122.5 4.4 %convolution_bitcast_fusion = f32[1024,1024]{0,1:T(8,128)} fusion(bf16[512,1024]{0,1:T(8,128)(2,1)} %all-gather.3.cloned.1.call-done, bf16[512,1024]{1,0:T(8,128)(2,1)S(1)} %copy-done), kind=kOutput, calls=%fused_computation.6 | convolution fusion | flops 1073741824 | bytes 6291456 | tf_op jit(solution)/shard_map/dot_general | solution.py:78
  126.9 6.7 %reshape.36 = f32[2,512,4,256]{1,0,3,2:T(2,128)} reshape(f32[1024,1024]{0,1:T(8,128)} %convolution_bitcast_fusion) | data formatting | bytes 8388608 | tf_op jit(solution)/shard_map/reshape | solution.py:84
  133.6 7.3 %copy.71 = f32[2,4,512,256]{3,2,1,0:T(8,128)} copy(f32[2,4,512,256]{2,0,3,1:T(2,128)} %bitcast.71) | data formatting | bytes 8388608 | tf_op jit(solution)/shard_map/transpose | solution.py:85
  142.0 18.7 %reduce-scatter.5.cloned.1.call-done = f32[512,256]{0,1:T(8,128)} async-done(((f32[512,1024]{0,1:T(8,128)}), f32[512,256]{0,1:T(8,128)}) %reduce-scatter.5.cloned.1.call-update) | async-done | bytes 524304 | tf_op jit(solution)/shard_map/reduce_scatter | solution.py:65
  161.6 3.4 %collective-permute-start.4 = (bf16[512,133]{0,1:T(8,128)(2,1)S(1)}, bf16[512,133]{0,1:T(8,128)(2,1)S(1)}, u32[]{:S(2)}, u32[]{:S(2)}) collective-permute-start(bf16[512,133]{0,1:T(8,128)(2,1)S(1)} %slice.138), channel_id=1, source_target_pairs={{8,0},{16,8},{24,16},{9,1},{17,9},{25,17},{10,2},{18,10},{26,18},{... | collective-permute-start | bytes 408584 | tf_op jit(solution)/shard_map/ppermute | solution.py:24
  165.0 4.7 %reduce-precision_reduce_fusion = bf16[512,1024]{1,0:T(8,128)(2,1)} fusion(bf16[512,4,256]{0,2,1:T(8,128)(2,1)} %bitcast.83, bf16[1024,4,256]{0,2,1:T(8,128)(2,1)} %bitcast.82), kind=kOutput, calls=%fused_computation | convolution fusion | flops 1079508992 | bytes 4194304 | tf_op jit(solution)/shard_map/dot_general | solution.py:95
  171.1 5.4 %fusion.18 = f32[1,512,262]{1,0,2:T(1,128)S(1)} fusion(f32[512,1,128]{0,1,2:T(1,128)S(1)} %copy.75, f32[1,512,389]{1,2,0:T(8,128)S(1)} %bitcast.73), kind=kOutput, calls=%fused_computation.32 | convolution fusion | flops 206045184 | bytes 1595392 | tf_op jit(solution)/shard_map/conv_general_dilated | solution.py:28
  178.1 2.4 reshape.69
  180.4 2.7 %pad.2 = f32[1536,1,264]{0,2,1:T(8,128)} pad(f32[1536,1,262]{0,2,1:T(8,128)} %reshape.69, f32[]{:T(128)} %constant.11.clone.1), padding=0_0x0_0x0_2 | pad | bytes 3231748 | tf_op jit(solution)/shard_map/broadcast_in_dim;reshape | solution.py:29
  183.2 3.2 %reshape.55 = f32[1536,1,8,33]{0,1,3,2:T(1,128)S(1)} reshape(f32[1536,1,264]{0,2,1:T(8,128)} %pad.2) | data formatting | bytes 3244032 | tf_op jit(solution)/shard_map/conv_general_dilated | solution.py:28
  189.2 23.6 %reduce-scatter.3.cloned.1.call-done = f32[512,256]{1,0:T(8,128)} async-done(((f32[4096,256]{1,0:T(8,128)}), f32[512,256]{1,0:T(8,128)}) %reduce-scatter.3.cloned.1.call-update) | async-done | bytes 524304 | tf_op jit(solution)/shard_map/reduce_scatter | solution.py:88
  217.1 17.6 %collective-permute-done.2 = bf16[512,256]{1,0:T(8,128)(2,1)S(1)} collective-permute-done((bf16[512,256]{1,0:T(8,128)(2,1)S(1)}, bf16[512,256]{1,0:T(8,128)(2,1)S(1)}, u32[]{:S(2)}, u32[]{:S(2)}) %collective-permute-start.2) | collective-permute-done | bytes 262176 | tf_op jit(solution)/shard_map/ppermute | solution.py:93
  (93 shorter events, 42.1 us)
Async XLA Ops:
  7.2 80.8 %copy-start = (bf16[512,1024]{1,0:T(8,128)(2,1)S(1)}, bf16[512,1024]{1,0:T(8,128)(2,1)}, u32[]{:S(2)}) copy-start(bf16[512,1024]{1,0:T(8,128)(2,1)} %param.10) | copy-start | bytes 3145732
  7.2 15.0 %all-to-all-start = ((bf16[4,128,256]{2,1,0:T(8,128)(2,1)}), bf16[4,128,256]{2,1,0:T(8,128)(2,1)S(1)}, u32[]{:S(2)}, u32[]{:S(2)}) async-start(bf16[4,128,256]{2,1,0:T(8,128)(2,1)} %bitcast.78), calls=%async_computation.1 | async-start | bytes 524288 | tf_op jit(solution)/shard_map/all_to_all | solution.py:43
  11.5 76.5 %all-gather.5.cloned.1.call-start = ((), (), s32[]{:S(2)}) async-start(), calls=%async_computation.5 | async-start | bytes 2359296 | tf_op jit(solution)/shard_map/all_gather | solution.py:51
  13.4 10.9 %copy-start.14 = (f32[3,512,7]{1,2,0:T(8,128)S(1)}, f32[3,512,7]{1,2,0:T(8,128)}, u32[]{:S(2)}) copy-start(f32[3,512,7]{1,2,0:T(8,128)} %param.7) | copy-start | bytes 129028
  13.4 11.2 %copy-start.10 = (f32[512,128]{1,0:T(8,128)S(1)}, f32[512,128]{1,0:T(8,128)}, u32[]{:S(2)}) copy-start(f32[512,128]{1,0:T(8,128)} %param.8) | copy-start | bytes 786436
  14.4 19.0 %collective-permute-start = (bf16[3,512,133]{1,2,0:T(8,128)(2,1)}, bf16[3,512,133]{1,2,0:T(8,128)(2,1)S(1)}, u32[]{:S(2)}, u32[]{:S(2)}) collective-permute-start(bf16[3,512,133]{1,2,0:T(8,128)(2,1)} %copy.89), channel_id=1, source_target_pairs={{0,8},{8,16},{16,24},{1,9},{9,17},{17,25},{2,10},{10,18},{18,26},{... | collective-permute-start | bytes 1225736 | tf_op jit(solution)/shard_map/ppermute | solution.py:13
  18.8 16.6 %collective-permute-start.1 = (bf16[3,512,133]{1,2,0:T(8,128)(2,1)}, bf16[3,512,133]{1,2,0:T(8,128)(2,1)S(1)}, u32[]{:S(2)}, u32[]{:S(2)}) collective-permute-start(bf16[3,512,133]{1,2,0:T(8,128)(2,1)} %copy.90), channel_id=1, source_target_pairs={{8,0},{16,8},{24,16},{9,1},{17,9},{25,17},{10,2},{18,10},{26,18},{... | collective-permute-start | bytes 1225736 | tf_op jit(solution)/shard_map/ppermute | solution.py:16
  22.3 14.2 %collective-permute-start.3 = (bf16[128,1024]{0,1:T(8,128)(2,1)S(1)}, bf16[128,1024]{0,1:T(8,128)(2,1)S(1)}, u32[]{:S(2)}, u32[]{:S(2)}) collective-permute-start(bf16[128,1024]{0,1:T(8,128)(2,1)S(1)} %bitcast.79), channel_id=1, source_target_pairs={{0,0},{1,4},{2,8},{3,12},{4,16},{5,20},{6,24},{7,28},{8,1},{9,5},{... | collective-permute-start | bytes 786440 | tf_op jit(solution)/shard_map/ppermute | solution.py:50
  37.3 85.2 %all-gather.3.cloned.1.call-start = ((), (), s32[]{:S(2)}) async-start(), calls=%async_computation.3 | async-start | bytes 1310720 | tf_op jit(solution)/shard_map/all_gather | solution.py:77
  59.2 2.3 copy-start.6
  61.5 1.2 copy-start.7
  62.7 23.5 %copy-start.2 = (f32[512,516]{0,1:T(8,128)}, f32[512,516]{0,1:T(8,128)S(1)}, u32[]{:S(2)}) copy-start(f32[512,516]{0,1:T(8,128)S(1)} %slice_bitcast_fusion.2) | copy-start | bytes 3170308
  62.7 2.0 copy-start.9
  62.7 2.0 copy-start.13
  64.7 21.2 %copy-start.15 = (f32[512]{0:T(512)S(1)}, f32[512]{0:T(512)}, u32[]{:S(2)}) copy-start(f32[512]{0:T(512)} %param.9) | copy-start | bytes 6148
  87.9 72.7 %reduce-scatter.5.cloned.1.call-start = ((), (), s32[]{:S(2)}) async-start(), calls=%async_computation.6 | async-start | bytes 2621440 | tf_op jit(solution)/shard_map/reduce_scatter | solution.py:65
  92.3 120.5 %reduce-scatter.3.cloned.1.call-start = ((), (), s32[]{:S(2)}) async-start(), calls=%async_computation.4 | async-start | bytes 4718592 | tf_op jit(solution)/shard_map/reduce_scatter | solution.py:88
  140.8 1.0 copy-start.11
  161.6 8.1 %collective-permute-start.4 = (bf16[512,133]{0,1:T(8,128)(2,1)S(1)}, bf16[512,133]{0,1:T(8,128)(2,1)S(1)}, u32[]{:S(2)}, u32[]{:S(2)}) collective-permute-start(bf16[512,133]{0,1:T(8,128)(2,1)S(1)} %slice.138), channel_id=1, source_target_pairs={{8,0},{16,8},{24,16},{9,1},{17,9},{25,17},{10,2},{18,10},{26,18},{... | collective-permute-start | bytes 408584 | tf_op jit(solution)/shard_map/ppermute | solution.py:24
  165.0 4.7 %copy-start.5 = (f32[512,389]{0,1:T(8,128)S(1)}, f32[512,389]{0,1:T(8,128)}, u32[]{:S(2)}) copy-start(f32[512,389]{0,1:T(8,128)} %copy-done.4) | copy-start | bytes 2390020
  165.0 4.7 %copy-start.8 = (f32[512,256]{0,1:T(8,128)S(1)}, f32[512,256]{0,1:T(8,128)}, u32[]{:S(2)}) copy-start(f32[512,256]{0,1:T(8,128)} %reduce-scatter.5.cloned.1.call-done) | copy-start | bytes 1572868
  169.7 1.2 copy-start.3
  212.8 22.6 %copy-start.1 = (bf16[512,1024]{1,0:T(8,128)(2,1)S(1)}, bf16[512,1024]{1,0:T(8,128)(2,1)}, u32[]{:S(2)}) copy-start(bf16[512,1024]{1,0:T(8,128)(2,1)} %param.10) | copy-start | bytes 3145732
  213.9 20.7 %collective-permute-start.2 = (bf16[512,256]{1,0:T(8,128)(2,1)S(1)}, bf16[512,256]{1,0:T(8,128)(2,1)S(1)}, u32[]{:S(2)}, u32[]{:S(2)}) collective-permute-start(bf16[512,256]{1,0:T(8,128)(2,1)S(1)} %convert_element_type.21), channel_id=1, source_target_pairs={{0,0},{1,8},{2,16},{3,24},{4,1},{5,9},{6,17},{7,25},{8,2},{9,10},{... | collective-permute-start | bytes 786440 | tf_op jit(solution)/shard_map/ppermute | solution.py:93
  (4 other events, 3.0 us)
Sparse Core Ops, SparseCore 0:
  37.4 38.2 all-gather.4
  88.1 34.3 all-gather.2
  125.4 35.1 reduce-scatter.4
  162.8 49.9 reduce-scatter.2
where the time goes:
time: 243 us; the launch traced here: 242 us
  waiting for transfers between devices  98.2 us (40%)
  local copies, waits for them, and re-layouts  60.3 us (25%)
  matrix products  43.1 us (18%)
  starting transfers between devices  18.8 us (8%)
  between operations  14.2 us (6%)
  other arithmetic  7.25 us (3%)
    all_gather x1, waiting for transfers between devices, shards(): gated_all = lax.all_gather(gated, 'seq', axis=1, tiled=True)  29.9 us
    conv_general_dilated x4, matrix products, correlate(): lax.conv_general_dilated(signal[None], taps[:, None, :], (1,), 'VALID', d...  29.8 us
    reduce_scatter x1, waiting for transfers between devices, shards(): lax.psum_scatter(partial_out, 'tp', scatter_dimension=0, tiled=True)  23.6 us
    reduce_scatter x1, waiting for transfers between devices, shards(): lax.psum_scatter(partial_grad, 'seq', scatter_dimension=1, tiled=True)  18.7 us
    ppermute x1, waiting for transfers between devices, shards(): mixed = lax.ppermute(output_sum.astype(jnp.bfloat16), ('seq', 'tp'), route)  17.6 us
    conv_general_dilated x12, local copies, waits for them, and re-layouts, correlate(): lax.conv_general_dilated(signal[None], taps[:, None, :], (1,), 'VALID', d...  13.3 us
    another operation x4, local copies, waits for them, and re-layouts, correlate(): signal[None]  9.99 us
    unnamed x39, local copies, waits for them, and re-layouts  8.37 us
  transfers between devices with their start and end apart: 10, of which 6 were waited for; matrix products, arithmetic and copies ran while one was open for 43% of the time, Pallas kernels for 0%

commit v1 on v0

--- a/solution.py
+++ b/solution.py
@@ -3,6 +3,12 @@
 import jax.numpy as jnp
 from jax import lax
 from jax.sharding import PartitionSpec as P
+
+
+def tiled_gather(x, axis, dim):
+    size = lax.axis_size(axis)
+    repeats = [size if d == dim else 1 for d in range(x.ndim)]
+    return lax.all_to_all(jnp.tile(x, repeats), axis, split_axis=dim, concat_axis=dim, tiled=True)
 
 
 def extended(block, sides, width):
@@ -74,7 +80,7 @@
     summed = convolved + skip_gain[:, None] * product[:, taps_long - 1 :]
     query_tail = query_feat[:, taps_long - 1 :]
     gated = (query_tail[:, :length] * summed[:, :length]).astype(jnp.bfloat16)
-    gated_all = lax.all_gather(gated, "seq", axis=1, tiled=True)
+    gated_all = tiled_gather(gated, "seq", 1)
     partial_out = lax.dot_general(
         out_weight, gated_all, (((0,), (0,)), ((), ())), preferred_element_type=jnp.float32
     )

time: 243 us -> 231 us (0.951)
  waiting for transfers between devices: 98.2 us -> 55.8 us
  blocking collectives: 0 us -> 28 us
  local copies, waits for them, and re-layouts: 60.3 us -> 63.9 us
    all_gather x1 -> x0, waiting for transfers between devices: 29.9 us -> none  [shards(): gated_all = lax.all_gather(gated, 'seq', axis=1, tiled=True)]
    all_to_all x0 -> x2, blocking collectives: none -> 28 us  [the longest x1 19 us: tiled_gather(): lax.all_to_all(jnp.tile(x, repeats), axis, split_axis=dim, concat_axis=di...]
    reduce_scatter x1, waiting for transfers between devices: 18.7 us -> 0.02 us  [shards(): lax.psum_scatter(partial_grad, 'seq', scatter_dimension=1, tiled=True)]
    ppermute x1, waiting for transfers between devices: 0.01 us -> 8.07 us  [rows_of_slab(): moved = lax.ppermute(mine, ('seq', 'tp'), route)]
    all_to_all x1 -> x0, starting transfers between devices: 4.36 us -> none  [rows_of_slab(): mine = lax.all_to_all(split, 'seq', 0, 0)]
    reduce_scatter x1, waiting for transfers between devices: 23.6 us -> 19.7 us  [shards(): lax.psum_scatter(partial_out, 'tp', scatter_dimension=0, tiled=True)]
    ppermute x1, waiting for transfers between devices: 0.83 us -> 3.41 us  [extended(): lax.ppermute(lax.slice_in_dim(block, 0, width, axis=dim), axis, backward)]
    unnamed x39 -> x45, local copies, waits for them, and re-layouts: 8.37 us -> 9.8 us
  transfers between devices with their start and end apart: 10 -> 8, of which waited for: 6 -> 5; matrix products, arithmetic and copies ran while one was open for 43% -> 44% of each run, Pallas kernels for 0% -> 0%
where the time goes in v1:
time: 231 us; the launch traced here: 230 us
  local copies, waits for them, and re-layouts  63.9 us (28%)
  waiting for transfers between devices  55.8 us (24%)
  matrix products  43.1 us (19%)
  blocking collectives  28 us (12%)
  starting transfers between devices  17.8 us (8%)
  between operations  14.2 us (6%)
  other arithmetic  7.23 us (3%)
    conv_general_dilated x4, matrix products, correlate(): lax.conv_general_dilated(signal[None], taps[:, None, :], (1,), 'VALID', d...  29.8 us
    reduce_scatter x1, waiting for transfers between devices, shards(): lax.psum_scatter(partial_out, 'tp', scatter_dimension=0, tiled=True)  19.7 us
    all_to_all x1, blocking collectives, tiled_gather(): lax.all_to_all(jnp.tile(x, repeats), axis, split_axis=dim, concat_axis=di...  19 us
    ppermute x1, waiting for transfers between devices, shards(): mixed = lax.ppermute(output_sum.astype(jnp.bfloat16), ('seq', 'tp'), route)  17.6 us
    conv_general_dilated x12, local copies, waits for them, and re-layouts, correlate(): lax.conv_general_dilated(signal[None], taps[:, None, :], (1,), 'VALID', d...  13.3 us
    another operation x4, local copies, waits for them, and re-layouts, correlate(): signal[None]  10.1 us
    unnamed x45, local copies, waits for them, and re-layouts  9.8 us
    all_to_all x1, blocking collectives, rows_of_slab(): mine = lax.all_to_all(split, 'seq', 0, 0)  8.98 us
  transfers between devices with their start and end apart: 8, of which 5 were waited for; matrix products, arithmetic and copies ran while one was open for 44% of the time, Pallas kernels for 0%

profile of v1, /device:TPU:4, one launch (start us, length us, event | category | flops | bytes accessed | tf_op | source)
XLA Modules:
  0.0 229.9 jit_solution(6504052412188928454)
XLA Ops:
  7.2 9.0 %all_to_all.14 = bf16[4,128,256]{2,1,0:T(8,128)(2,1)S(1)} all-to-all(bf16[4,128,256]{2,1,0:T(8,128)(2,1)} %bitcast.79), channel_id=1, replica_groups=mesh['seq'=4,'tp'=8] {'seq'}, dimensions={0} | all-to-all | bytes 524288 | tf_op jit(solution)/shard_map/all_to_all | solution.py:49
  16.4 4.0 %collective-permute-start.3 = (bf16[128,1024]{0,1:T(8,128)(2,1)S(1)}, bf16[128,1024]{0,1:T(8,128)(2,1)S(1)}, u32[]{:S(2)}, u32[]{:S(2)}) collective-permute-start(bf16[128,1024]{0,1:T(8,128)(2,1)S(1)} %bitcast.80), channel_id=1, source_target_pairs={{0,0},{1,4},{2,8},{3,12},{4,16},{5,20},{6,24},{7,28},{8,1},{9,5},{... | collective-permute-start | bytes 786440 | tf_op jit(solution)/shard_map/ppermute | solution.py:56
  20.4 8.1 %collective-permute-done.3 = bf16[128,1024]{0,1:T(8,128)(2,1)S(1)} collective-permute-done((bf16[128,1024]{0,1:T(8,128)(2,1)S(1)}, bf16[128,1024]{0,1:T(8,128)(2,1)S(1)}, u32[]{:S(2)}, u32[]{:S(2)}) %collective-permute-start.3) | collective-permute-done | bytes 262176 | tf_op jit(solution)/shard_map/ppermute | solution.py:56
  30.7 4.7 %collective-permute-start = (bf16[3,512,133]{1,2,0:T(8,128)(2,1)}, bf16[3,512,133]{1,2,0:T(8,128)(2,1)S(1)}, u32[]{:S(2)}, u32[]{:S(2)}) collective-permute-start(bf16[3,512,133]{1,2,0:T(8,128)(2,1)} %copy.91), channel_id=1, source_target_pairs={{0,8},{8,16},{16,24},{1,9},{9,17},{17,25},{2,10},{10,18},{18,26},{... | collective-permute-start | bytes 1225736 | tf_op jit(solution)/shard_map/ppermute | solution.py:19
  35.6 3.3 %collective-permute-start.1 = (bf16[3,512,133]{1,2,0:T(8,128)(2,1)S(1)}, bf16[3,512,133]{1,2,0:T(8,128)(2,1)S(1)}, u32[]{:S(2)}, u32[]{:S(2)}) collective-permute-start(bf16[3,512,133]{1,2,0:T(8,128)(2,1)S(1)} %copy.92), channel_id=1, source_target_pairs={{8,0},{16,8},{24,16},{9,1},{17,9},{25,17},{10,2},{18,10},{26,18},{... | collective-permute-start | bytes 1225736 | tf_op jit(solution)/shard_map/ppermute | solution.py:22
  40.5 6.9 %collective-permute-done = bf16[3,512,133]{1,2,0:T(8,128)(2,1)S(1)} collective-permute-done((bf16[3,512,133]{1,2,0:T(8,128)(2,1)}, bf16[3,512,133]{1,2,0:T(8,128)(2,1)S(1)}, u32[]{:S(2)}, u32[]{:S(2)}) %collective-permute-start) | collective-permute-done | bytes 408608 | tf_op jit(solution)/shard_map/ppermute | solution.py:19
  48.6 3.4 %collective-permute-done.1 = bf16[3,512,133]{1,2,0:T(8,128)(2,1)S(1)} collective-permute-done((bf16[3,512,133]{1,2,0:T(8,128)(2,1)S(1)}, bf16[3,512,133]{1,2,0:T(8,128)(2,1)S(1)}, u32[]{:S(2)}, u32[]{:S(2)}) %collective-permute-start.1) | collective-permute-done | bytes 408608 | tf_op jit(solution)/shard_map/ppermute | solution.py:22
  53.1 2.5 %pad_maximum_fusion = bf16[3,512,522]{2,1,0:T(8,128)(2,1)S(1)} fusion(bf16[3,512,133]{2,1,0:T(8,128)(2,1)} %copy.63, bf16[3,512,256]{2,1,0:T(8,128)(2,1)} %param.6, bf16[3,512,133]{2,1,0:T(8,128)(2,1)} %copy.62), kind=kLoop, calls=%fused_computation.7 | loop fusion | flops 4810752 | bytes 3207168 | tf_op jit(solution)/shard_map/concatenate | solution.py:23
  55.7 2.3 %copy.64 = bf16[1536,1,522]{0,2,1:T(8,128)(2,1)} copy(bf16[1536,1,522]{2,0,1:T(8,128)(2,1)S(1)} %bitcast.72) | data formatting | bytes 3207168 | tf_op jit(solution)/shard_map/broadcast_in_dim;reshape | solution.py:35
  58.0 2.7 %pad = bf16[1536,1,528]{0,2,1:T(8,128)(2,1)} pad(bf16[1536,1,522]{0,2,1:T(8,128)(2,1)} %copy.64, bf16[]{:T(256)} %constant.12), padding=0_0x0_0x0_6 | pad | bytes 3225602 | tf_op jit(solution)/shard_map/broadcast_in_dim;reshape | solution.py:35
  64.1 4.2 %fusion.37 = f32[512,1024]{0,1:T(8,128)} fusion(bf16[512,1024]{1,0:T(8,128)(2,1)S(1)} %copy-done, bf16[1024,1024]{0,1:T(8,128)(2,1)} %all-gather.2.cloned.1.call-done), kind=kOutput, calls=%fused_computation.58 | convolution fusion | flops 1073741824 | bytes 5242880 | tf_op jit(solution)/shard_map/dot_general | solution.py:70
  87.3 21.1 %fusion.36 = f32[1,512,389]{1,0,2:T(1,128)S(1)} fusion(f32[1,528,512]{2,0,1:T(1,128)S(1)} %copy-done.12, f32[512,1,128]{0,1,2:T(1,128)S(1)} %copy-done.15), kind=kOutput, calls=%fused_computation.57 | convolution fusion | flops 305922048 | bytes 2140160 | tf_op jit(solution)/shard_map/conv_general_dilated | solution.py:34
  111.6 19.0 %all_to_all.15 = bf16[512,4,256]{2,0,1:T(8,128)(2,1)} all-to-all(bf16[512,4,256]{2,0,1:T(8,128)(2,1)S(1)} %tile.2), channel_id=1, replica_groups=mesh['seq'=4,'tp'=8] {'seq'}, dimensions={1} | all-to-all | bytes 2097152 | tf_op jit(solution)/shard_map/all_to_all | solution.py:11
  132.9 4.4 %convolution_bitcast_fusion = f32[1024,1024]{0,1:T(8,128)} fusion(bf16[512,1024]{0,1:T(8,128)(2,1)} %bitcast.74, bf16[512,1024]{1,0:T(8,128)(2,1)S(1)} %copy-done), kind=kOutput, calls=%fused_computation.6 | convolution fusion | flops 1073741824 | bytes 6291456 | tf_op jit(solution)/shard_map/dot_general | solution.py:84
  137.3 6.7 %reshape.42 = f32[2,512,4,256]{1,0,3,2:T(2,128)} reshape(f32[1024,1024]{0,1:T(8,128)} %convolution_bitcast_fusion) | data formatting | bytes 8388608 | tf_op jit(solution)/shard_map/reshape | solution.py:90
  144.0 7.3 %copy.75 = f32[2,4,512,256]{3,2,1,0:T(8,128)} copy(f32[2,4,512,256]{2,0,3,1:T(2,128)} %bitcast.71) | data formatting | bytes 8388608 | tf_op jit(solution)/shard_map/transpose | solution.py:91
  153.4 3.6 %collective-permute-start.4 = (bf16[512,133]{0,1:T(8,128)(2,1)S(1)}, bf16[512,133]{0,1:T(8,128)(2,1)S(1)}, u32[]{:S(2)}, u32[]{:S(2)}) collective-permute-start(bf16[512,133]{0,1:T(8,128)(2,1)S(1)} %slice.138), channel_id=1, source_target_pairs={{8,0},{16,8},{24,16},{9,1},{17,9},{25,17},{10,2},{18,10},{26,18},{... | collective-permute-start | bytes 408584 | tf_op jit(solution)/shard_map/ppermute | solution.py:30
  157.0 4.6 %reduce-precision_reduce_fusion = bf16[512,1024]{1,0:T(8,128)(2,1)} fusion(bf16[512,4,256]{2,0,1:T(8,128)(2,1)} %all_to_all.15, bf16[1024,4,256]{0,2,1:T(8,128)(2,1)} %bitcast.83), kind=kOutput, calls=%fused_computation | convolution fusion | flops 1079508992 | bytes 4194304 | tf_op jit(solution)/shard_map/dot_general | solution.py:101
  163.0 5.4 %fusion.18 = f32[1,512,262]{1,0,2:T(1,128)S(1)} fusion(f32[512,1,128]{0,1,2:T(1,128)S(1)} %copy.79, f32[1,512,389]{1,2,0:T(8,128)S(1)} %bitcast.73), kind=kOutput, calls=%fused_computation.32 | convolution fusion | flops 206045184 | bytes 1595392 | tf_op jit(solution)/shard_map/conv_general_dilated | solution.py:34
  170.0 2.4 %reshape.74 = f32[1536,1,262]{0,2,1:T(8,128)} reshape(f32[3,512,262]{1,0,2:T(4,128)S(1)} %copy.80) | data formatting | bytes 3219456 | tf_op jit(solution)/shard_map/broadcast_in_dim;reshape | solution.py:35
  172.4 2.7 %pad.2 = f32[1536,1,264]{0,2,1:T(8,128)} pad(f32[1536,1,262]{0,2,1:T(8,128)} %reshape.74, f32[]{:T(128)} %constant.11.clone.1), padding=0_0x0_0x0_2 | pad | bytes 3231748 | tf_op jit(solution)/shard_map/broadcast_in_dim;reshape | solution.py:35
  175.1 3.3 %reshape.60 = f32[1536,1,8,33]{0,1,3,2:T(1,128)S(1)} reshape(f32[1536,1,264]{0,2,1:T(8,128)} %pad.2) | data formatting | bytes 3244032 | tf_op jit(solution)/shard_map/conv_general_dilated | solution.py:34
  181.1 19.7 %reduce-scatter.3.cloned.1.call-done = f32[512,256]{1,0:T(8,128)} async-done(((f32[4096,256]{1,0:T(8,128)}), f32[512,256]{1,0:T(8,128)}) %reduce-scatter.3.cloned.1.call-update) | async-done | bytes 524304 | tf_op jit(solution)/shard_map/reduce_scatter | solution.py:94
  205.1 17.6 %collective-permute-done.2 = bf16[512,256]{1,0:T(8,128)(2,1)S(1)} collective-permute-done((bf16[512,256]{1,0:T(8,128)(2,1)S(1)}, bf16[512,256]{1,0:T(8,128)(2,1)S(1)}, u32[]{:S(2)}, u32[]{:S(2)}) %collective-permute-start.2) | collective-permute-done | bytes 262176 | tf_op jit(solution)/shard_map/ppermute | solution.py:99
  (99 shorter events, 46.8 us)
Async XLA Ops:
  7.2 57.0 %copy-start = (bf16[512,1024]{1,0:T(8,128)(2,1)S(1)}, bf16[512,1024]{1,0:T(8,128)(2,1)}, u32[]{:S(2)}) copy-start(bf16[512,1024]{1,0:T(8,128)(2,1)} %param.10) | copy-start | bytes 3145732
  7.2 22.1 %copy-start.2 = (bf16[3,512,256]{2,1,0:T(8,128)(2,1)S(1)}, bf16[3,512,256]{2,1,0:T(8,128)(2,1)}, u32[]{:S(2)}) copy-start(bf16[3,512,256]{2,1,0:T(8,128)(2,1)} %param.6) | copy-start | bytes 2359300
  7.2 56.9 %all-gather.2.cloned.1.call-start = ((), (), s32[]{:S(2)}) async-start(), calls=%async_computation.5 | async-start | bytes 2359296 | tf_op jit(solution)/shard_map/all_gather | solution.py:57
  16.4 12.1 %collective-permute-start.3 = (bf16[128,1024]{0,1:T(8,128)(2,1)S(1)}, bf16[128,1024]{0,1:T(8,128)(2,1)S(1)}, u32[]{:S(2)}, u32[]{:S(2)}) collective-permute-start(bf16[128,1024]{0,1:T(8,128)(2,1)S(1)} %bitcast.80), channel_id=1, source_target_pairs={{0,0},{1,4},{2,8},{3,12},{4,16},{5,20},{6,24},{7,28},{8,1},{9,5},{... | collective-permute-start | bytes 786440 | tf_op jit(solution)/shard_map/ppermute | solution.py:56
  29.2 123.1 %reduce-scatter.5.cloned.1.call-start = ((), (), s32[]{:S(2)}) async-start(), calls=%async_computation.6 | async-start | bytes 2621440 | tf_op jit(solution)/shard_map/reduce_scatter | solution.py:71
  29.6 9.2 %copy-start.17 = (f32[3,512,7]{1,2,0:T(8,128)S(1)}, f32[3,512,7]{1,2,0:T(8,128)}, u32[]{:S(2)}) copy-start(f32[3,512,7]{1,2,0:T(8,128)} %param.7) | copy-start | bytes 129028
  29.7 9.6 %copy-start.13 = (f32[512,128]{1,0:T(8,128)S(1)}, f32[512,128]{1,0:T(8,128)}, u32[]{:S(2)}) copy-start(f32[512,128]{1,0:T(8,128)} %param.8) | copy-start | bytes 786436
  30.7 16.7 %collective-permute-start = (bf16[3,512,133]{1,2,0:T(8,128)(2,1)}, bf16[3,512,133]{1,2,0:T(8,128)(2,1)S(1)}, u32[]{:S(2)}, u32[]{:S(2)}) collective-permute-start(bf16[3,512,133]{1,2,0:T(8,128)(2,1)} %copy.91), channel_id=1, source_target_pairs={{0,8},{8,16},{16,24},{1,9},{9,17},{17,25},{2,10},{10,18},{18,26},{... | collective-permute-start | bytes 1225736 | tf_op jit(solution)/shard_map/ppermute | solution.py:19
  35.6 16.4 %collective-permute-start.1 = (bf16[3,512,133]{1,2,0:T(8,128)(2,1)S(1)}, bf16[3,512,133]{1,2,0:T(8,128)(2,1)S(1)}, u32[]{:S(2)}, u32[]{:S(2)}) collective-permute-start(bf16[3,512,133]{1,2,0:T(8,128)(2,1)S(1)} %copy.92), channel_id=1, source_target_pairs={{8,0},{16,8},{24,16},{9,1},{17,9},{25,17},{10,2},{18,10},{26,18},{... | collective-permute-start | bytes 1225736 | tf_op jit(solution)/shard_map/ppermute | solution.py:22
  68.4 1.4 copy-start.11
  68.4 1.4 copy-start.19
  68.4 132.4 %reduce-scatter.3.cloned.1.call-start = ((), (), s32[]{:S(2)}) async-start(), calls=%async_computation.4 | async-start | bytes 4718592 | tf_op jit(solution)/shard_map/reduce_scatter | solution.py:94
  81.6 2.3 %copy-start.7 = (f32[1,528,512]{2,1,0:T(8,128)S(1)}, f32[1,528,512]{2,1,0:T(8,128)}, u32[]{:S(2)}) copy-start(f32[1,528,512]{2,1,0:T(8,128)} %reshape.53) | copy-start | bytes 3244036
  83.9 1.3 copy-start.8
  85.2 23.6 %copy-start.3 = (f32[512,516]{0,1:T(8,128)}, f32[512,516]{0,1:T(8,128)S(1)}, u32[]{:S(2)}) copy-start(f32[512,516]{0,1:T(8,128)S(1)} %slice_bitcast_fusion.2) | copy-start | bytes 3170308
  85.2 2.0 copy-start.12
  85.2 2.1 copy-start.15
  87.3 21.2 %copy-start.18 = (f32[512]{0:T(512)S(1)}, f32[512]{0:T(512)}, u32[]{:S(2)}) copy-start(f32[512]{0:T(512)} %param.9) | copy-start | bytes 6148
  153.4 8.3 %collective-permute-start.4 = (bf16[512,133]{0,1:T(8,128)(2,1)S(1)}, bf16[512,133]{0,1:T(8,128)(2,1)S(1)}, u32[]{:S(2)}, u32[]{:S(2)}) collective-permute-start(bf16[512,133]{0,1:T(8,128)(2,1)S(1)} %slice.138), channel_id=1, source_target_pairs={{8,0},{16,8},{24,16},{9,1},{17,9},{25,17},{10,2},{18,10},{26,18},{... | collective-permute-start | bytes 408584 | tf_op jit(solution)/shard_map/ppermute | solution.py:30
  157.0 4.7 %copy-start.6 = (f32[512,389]{0,1:T(8,128)S(1)}, f32[512,389]{0,1:T(8,128)}, u32[]{:S(2)}) copy-start(f32[512,389]{0,1:T(8,128)} %copy-done.5) | copy-start | bytes 2390020
  157.0 4.7 %copy-start.9 = (f32[512,256]{0,1:T(8,128)S(1)}, f32[512,256]{0,1:T(8,128)}, u32[]{:S(2)}) copy-start(f32[512,256]{0,1:T(8,128)} %reduce-scatter.5.cloned.1.call-done) | copy-start | bytes 1572868
  161.6 1.2 copy-start.4
  200.8 22.6 %copy-start.1 = (bf16[512,1024]{1,0:T(8,128)(2,1)S(1)}, bf16[512,1024]{1,0:T(8,128)(2,1)}, u32[]{:S(2)}) copy-start(bf16[512,1024]{1,0:T(8,128)(2,1)} %param.10) | copy-start | bytes 3145732
  202.0 20.7 %collective-permute-start.2 = (bf16[512,256]{1,0:T(8,128)(2,1)S(1)}, bf16[512,256]{1,0:T(8,128)(2,1)S(1)}, u32[]{:S(2)}, u32[]{:S(2)}) collective-permute-start(bf16[512,256]{1,0:T(8,128)(2,1)S(1)} %convert_element_type.21), channel_id=1, source_target_pairs={{0,0},{1,8},{2,16},{3,24},{4,1},{5,9},{6,17},{7,25},{8,2},{9,10},{... | collective-permute-start | bytes 786440 | tf_op jit(solution)/shard_map/ppermute | solution.py:99
  (5 other events, 4.4 us)
Sparse Core Ops, SparseCore 0:
  29.3 32.7 all-gather.1
  68.5 37.1 reduce-scatter.4
  151.4 49.3 reduce-scatter.2
